TPU v7x, 128 devices: a whole 4x4x4 slice. The times are simulated.
128 devices in a mesh: req: 16 (over y, x), kv: 8 (over z, core).
Axes of the slice: x: 4, y: 4, z: 4, core: 2. Of those that a mesh axis runs over, the one named last changes fastest.
Arguments:
- hidden: bfloat16 [1024, 1536], P('req', 'kv'), may hold values from -6 to 6
- perm: int32 [1024], replicated, may hold values from 0 to 1023, as said below
- seq_lens: int32 [1024], P('req'), may hold values from 1 to 4096, as said below
- page_table: int32 [1024, 32], P('req'), may hold values from 0 to 319, as said below
- kv_cache: bfloat16 [5120, 8, 128, 128], P('req', 'kv'), may hold values from -52 to 52
- attn_gain: float32 [1536], replicated, may hold values from 0.1 to 1.9
- qkv_weight: bfloat16 [8, 1536, 320], P('kv'), may hold values from -0.15625 to 0.15625
- out_weight: bfloat16 [8, 192, 1536], P('kv'), may hold values from -1 to 1
- ffn_gain: float32 [1536], replicated, may hold values from 0.1 to 1.9
- router: bfloat16 [1536, 16], replicated, may hold values from -0.15625 to 0.15625
- routes: int32 [1024, 2], P(('req', 'kv')), may hold values from 0 to 15, all different within a row; in each aligned block of 8 rows (0 to 7, 8 to 15, ...) at most 2 rows name the same one
- gate_up: bfloat16 [16, 1536, 2048], P('req'), may hold values from -0.15625 to 0.15625
- down: bfloat16 [16, 1024, 1536], P('req'), may hold values from -0.1875 to 0.1875
Outputs:
- mixed: bfloat16 [1024, 1536], P(('req', 'kv'))
Inputs may be any that keep to these rules, and one draw needn't show every extreme that they name: A permutation of the 1024 requests: slot s holds request perm[s]. The 64 slots of each index of req hold exactly 4 requests from each block of 64 consecutive requests. `seq_lens`: the length 4096 is reached on every index of req. `page_table`: entries 0 to (seq_lens[s] + 127) // 128 - 1 of row s are used; no page of one index of req is used by two of its slots; later entries name arbitrary pages.
All inputs are finite; a program needn't handle non-finite values.
Results may differ from a plain program's by a relative error of at most 0.017.
Values may be sent and summed in bfloat16 or wider, within the bound.
No kernel may reach another device: no remote copies, remote signals or barrier semaphores. Data moves between devices by JAX's collectives and lax.ppermute only.
A program may use at most 128 MiB of HBM per device.

v0:
```python
import jax
import jax.numpy as jnp
from jax import lax
from jax.sharding import PartitionSpec as P

REQ_DEV = 64
NEG_FILL = -1e30
EPS_NORM = 1e-05


def rms_norm(values, gain_vec):
    values = values.astype(jnp.float32)
    factor = lax.rsqrt(jnp.mean(values * values, axis=-1, keepdims=True) + EPS_NORM)
    return (values * factor * gain_vec).astype(jnp.bfloat16)


def attend(normed, seq_lens, page_table, kv_cache, qkv_weight):
    pool_pages, local_heads, twice_hd, page_len = kv_cache.shape
    head_dim = twice_hd // 2
    slot_count = normed.shape[0]
    groups = qkv_weight.shape[2] // head_dim - 2
    max_pages = page_table.shape[1]
    projected = jnp.einsum("sd,hdc->shc", normed, qkv_weight, preferred_element_type=jnp.float32)
    queries = (
        projected[:, :, : groups * head_dim]
        .reshape(slot_count, local_heads, groups, head_dim)
        .astype(jnp.bfloat16)
    )
    key_new = projected[:, :, groups * head_dim : (groups + 1) * head_dim].astype(jnp.bfloat16)
    value_new = projected[:, :, (groups + 1) * head_dim :].astype(jnp.bfloat16)
    page_need = (seq_lens + page_len - 1) // page_len
    page_ids = jnp.arange(max_pages, dtype=jnp.int32)
    in_use = page_ids[None, :] < page_need[:, None]
    pool_ids = jnp.arange(pool_pages, dtype=jnp.int32)
    match = (page_table[:, :, None] == pool_ids[None, None, :]) & in_use[:, :, None]
    belongs = jnp.any(match, axis=1)
    page_order = jnp.sum(jnp.where(match, page_ids[None, :, None], 0), axis=(0, 1))
    owner_len = jnp.sum(jnp.where(belongs, seq_lens[:, None], 0), axis=0)
    position = page_order[:, None] * page_len + jnp.arange(page_len, dtype=jnp.int32)[None, :]
    live = position < owner_len[:, None]
    scale_factor = head_dim ** (-0.5)
    page_queries = (
        jnp.dot(
            belongs.T.astype(jnp.bfloat16),
            queries.reshape(slot_count, -1),
            preferred_element_type=jnp.float32,
        )
        .astype(jnp.bfloat16)
        .reshape(pool_pages, local_heads, groups, head_dim)
    )
    scores = (
        jnp.einsum(
            "pkgd,pkdt->pkgt",
            page_queries,
            kv_cache[:, :, :head_dim, :],
            preferred_element_type=jnp.float32,
        )
        * scale_factor
    )
    scores = jnp.where(live[:, None, None, :], scores, NEG_FILL)
    score_new = (
        jnp.einsum("skgd,skd->skg", queries, key_new, preferred_element_type=jnp.float32)
        * scale_factor
    )
    page_peak = jnp.max(scores, axis=3)
    slot_peak = jnp.max(jnp.where(belongs[:, :, None, None], page_peak[None], NEG_FILL), axis=1)
    slot_peak = jnp.maximum(slot_peak, score_new)
    page_peak_of_owner = jnp.max(
        jnp.where(belongs[:, :, None, None], slot_peak[:, None], NEG_FILL), axis=0
    )
    weights = jnp.where(
        live[:, None, None, :], jnp.exp(scores - page_peak_of_owner[..., None]), 0.0
    )
    page_total = jnp.sum(weights, axis=3)
    page_value = jnp.einsum(
        "pkgt,pkdt->pkgd",
        weights.astype(jnp.bfloat16),
        kv_cache[:, :, head_dim:, :],
        preferred_element_type=jnp.float32,
    )
    belongs_f = belongs.astype(jnp.float32)
    total_sum = jnp.dot(
        belongs_f, page_total.reshape(pool_pages, -1), precision=lax.Precision.HIGHEST
    ).reshape(slot_count, local_heads, groups)
    value_sum = jnp.dot(
        belongs_f, page_value.reshape(pool_pages, -1), precision=lax.Precision.HIGHEST
    ).reshape(slot_count, local_heads, groups, head_dim)
    weight_new = jnp.exp(score_new - slot_peak)
    total_sum = total_sum + weight_new
    rounded_new = lax.optimization_barrier(weight_new.astype(jnp.bfloat16)).astype(jnp.float32)
    value_sum = value_sum + rounded_new[..., None] * value_new.astype(jnp.float32)[:, :, None, :]
    return (value_sum / total_sum[..., None]).astype(jnp.bfloat16).reshape(slot_count, -1)


def expert_apply(piece, gate_up, down):
    n_source, slot_num, local_experts, width = piece.shape
    rows_in = piece.transpose(2, 0, 1, 3).reshape(local_experts, n_source * slot_num, width)
    projected_up = jnp.einsum("erd,edf->erf", rows_in, gate_up, preferred_element_type=jnp.float32)
    hidden_units = gate_up.shape[2] // 2
    acts = (
        jax.nn.silu(projected_up[..., :hidden_units]) * projected_up[..., hidden_units:]
    ).astype(jnp.bfloat16)
    result = jnp.einsum("erf,efd->erd", acts, down, preferred_element_type=jnp.float32).astype(
        jnp.bfloat16
    )
    return result.reshape(local_experts, n_source, slot_num, width).transpose(1, 2, 0, 3)


def shards(
    hidden,
    perm,
    seq_lens,
    page_table,
    kv_cache,
    attn_gain,
    qkv_weight,
    out_weight,
    ffn_gain,
    router,
    routes,
    gate_up,
    down,
):
    req_index = lax.axis_index("req")
    kv_index = lax.axis_index("kv")
    every_row = lax.all_gather(hidden, "req", axis=0, tiled=True)
    my_perm = lax.dynamic_slice_in_dim(perm, req_index * REQ_DEV, REQ_DEV)
    pick = (my_perm[:, None] == jnp.arange(every_row.shape[0], dtype=jnp.int32)[None, :]).astype(
        every_row.dtype
    )
    picked_rows = jnp.dot(pick, every_row, preferred_element_type=jnp.float32).astype(
        every_row.dtype
    )
    tokens = lax.all_gather(picked_rows, "kv", axis=1, tiled=True)
    normed = rms_norm(tokens, attn_gain)
    head_out = attend(normed, seq_lens, page_table, kv_cache, qkv_weight)
    sub_rows = routes.shape[0]
    width = tokens.shape[1]
    out_flat = out_weight.reshape(-1, out_weight.shape[2])
    attn_rows = lax.psum_scatter(
        jnp.dot(head_out, out_flat, preferred_element_type=jnp.float32).astype(jnp.bfloat16),
        "kv",
        scatter_dimension=0,
        tiled=True,
    ).astype(jnp.float32)
    own_tokens = lax.dynamic_slice_in_dim(tokens, kv_index * sub_rows, sub_rows, 0)
    residual = (own_tokens.astype(jnp.float32) + attn_rows).astype(jnp.bfloat16)
    normed_ffn = rms_norm(residual, ffn_gain)
    logits = jnp.dot(normed_ffn, router, preferred_element_type=jnp.float32)
    chosen = jnp.take_along_axis(logits, routes, axis=1)
    sigmoid_vals = jax.nn.sigmoid(chosen)
    gates = sigmoid_vals / jnp.sum(sigmoid_vals, axis=1, keepdims=True)
    experts_all = router.shape[1]
    n_req = lax.axis_size("req")
    local_experts = gate_up.shape[0]
    capacity = max(2, 2 * sub_rows // experts_all + 1)
    flat_routes = routes.reshape(-1)
    onehot_int = (flat_routes[:, None] == jnp.arange(experts_all, dtype=jnp.int32)[None, :]).astype(
        jnp.int32
    )
    earlier = jnp.cumsum(onehot_int, axis=0) - onehot_int
    rank_in = jnp.sum(earlier * onehot_int, axis=1)
    place_at = (
        flat_routes // local_experts * capacity * local_experts
        + rank_in * local_experts
        + flat_routes % local_experts
    )
    placement_plan = (
        place_at[:, None] == jnp.arange(experts_all * capacity, dtype=jnp.int32)[None, :]
    ).astype(jnp.bfloat16)
    paired_rows = jnp.repeat(normed_ffn, 2, axis=0)
    outgoing = jnp.einsum(
        "qe,qd->ed", placement_plan, paired_rows, preferred_element_type=jnp.float32
    )
    outgoing = outgoing.astype(jnp.bfloat16).reshape(n_req, capacity, local_experts, width)
    arrived = lax.all_to_all(outgoing, "req", split_axis=0, concat_axis=0, tiled=True)
    returned = lax.all_to_all(
        expert_apply(arrived, gate_up, down), "req", split_axis=0, concat_axis=0, tiled=True
    )
    back_rows = returned.reshape(experts_all * capacity, width)
    paired_output = jnp.dot(placement_plan, back_rows, preferred_element_type=jnp.float32).reshape(
        sub_rows, 2, width
    )
    mixed = residual.astype(jnp.float32) + jnp.sum(gates[:, :, None] * paired_output, axis=1)
    return mixed.astype(jnp.bfloat16)


def solution(mesh):
    in_specs = (
        P("req", "kv"),
        P(),
        P("req"),
        P("req", None),
        P("req", "kv", None, None),
        P(),
        P("kv", None, None),
        P("kv", None, None),
        P(),
        P(),
        P(("req", "kv"), None),
        P("req", None, None),
        P("req", None, None),
    )
    out_specs = P(("req", "kv"), None)
    return jax.shard_map(shards, mesh=mesh, in_specs=in_specs, out_specs=out_specs, check_vma=False)
```

profile of v0, /device:TPU:0, one launch (start us, length us, event | category | flops | bytes accessed | tf_op | source)
XLA Modules:
  0.0 153.1 jit_solution(15035684609703527632)
XLA Ops:
  6.5 0.9 copy.88
  7.5 0.7 and_select_fusion
  8.2 0.9 fusion.7
  9.1 0.8 select_reduce_fusion
  10.0 26.8 %all_gather.6 = bf16[1024,192]{1,0:T(8,128)(2,1)} all-gather(bf16[64,192]{1,0:T(8,128)(2,1)} %param.13), channel_id=1, replica_groups=mesh['req'=16,'kv'=8] {'req'}, dimensions={0}, use_global_device_ids=true | all-gather | bytes 417792 | tf_op jit(solution)/shard_map/all_gather | solution.py:126
  36.8 0.8 dynamic_slice.6
  37.6 1.3 fusion.19
  38.9 14.0 %all-gather = bf16[8,192,64]{1,2,0:T(8,128)(2,1)S(1)} all-gather(bf16[1,192,64]{1,2,0:T(8,128)(2,1)S(1)} %fusion.19), channel_id=1, replica_groups=mesh['req'=16,'kv'=8] {'kv'}, dimensions={0}, use_global_device_ids=true | all-gather | bytes 221184 | tf_op jit(solution)/shard_map/all_gather | solution.py:134
  52.9 0.8 copy.87
  53.7 1.2 reshape.301
  54.9 0.1 fusion.24
  55.1 0.8 select_reduce_fusion.3
  55.8 1.6 %convolution_bitcast_fusion = bf16[64,1,320]{2,0,1:T(8,128)(2,1)S(1)} fusion(bf16[1,1536,320]{1,2,0:T(8,128)(2,1)} %param.19, bf16[1536,64]{0,1:T(8,128)(2,1)S(1)} %reshape.301, f32[1536]{0:T(1024)} %param.18, f32[64]{0:T(128)S(1)} %add_rsqrt_fusion.1), kind=kOutput, calls=%fused_computation.20 | convolution fusion | flops 63307776 | bytes 1227008 | tf_op jit(solution)/shard_map/sd,hdc->shc/dot_general | solution.py:23
  57.5 0.2 convolution_convert_fusion.2
  57.7 0.7 fusion.47
  58.4 0.9 copy.90
  59.4 0.2 add_compare_fusion
  59.5 5.6 %fusion.57 = (f32[320,3]{1,0:T(8,128)}, f32[320,3,128]{2,1,0:T(4,128)}) fusion(bf16[320,3,64]{2,1,0:T(4,128)(2,1)} %copy.90, bf16[320,1,128,128]{3,2,0,1:T(8,128)(2,1)} %bitcast.113, pred[320,128]{1,0:T(8,128)(4,1)S(1)} %add_compare_fusion), kind=kOutput, calls=%fused_computation.102 | convolution fusion | flops 16096320 | bytes 6106880 | tf_op jit(solution)/shard_map/pkgd,pkdt->pkgt/dot_general | solution.py:52
  65.2 1.0 copy.91
  66.2 0.1 select_reduce_fusion.2
  66.4 0.1 copy.114
  66.6 0.1 select_reduce_fusion.1
  66.7 0.1 copy.93
  66.9 1.9 %fusion.22 = f32[320,3]{1,0:T(8,128)S(1)} fusion(f32[320,3,128]{2,1,0:T(4,128)} %get-tuple-element.14, f32[320,3]{1,0:T(8,128)S(1)} %copy.93, pred[320,128]{1,0:T(8,128)(4,1)} %copy-done.2), kind=kLoop, calls=%fused_computation.34 | loop fusion | flops 367680 | bytes 540160 | tf_op jit(solution)/shard_map/reduce_sum | solution.py:74
  68.8 6.5 %fusion.2 = f32[320,3,64]{2,1,0:T(4,128)} fusion(bf16[320,1,128,128]{3,2,0,1:T(8,128)(2,1)} %bitcast.114, f32[320,3,128]{2,1,0:T(4,128)} %get-tuple-element.14, f32[320,3]{1,0:T(8,128)S(1)} %copy.93, pred[320,128]{1,0:T(8,128)(4,1)} %copy-done.2), kind=kOutput, calls=%fused_computation.4 | convolution fusion | flops 16097280 | bytes 6188800 | tf_op jit(solution)/shard_map/pkgt,pkdt->pkgd/dot_general | solution.py:75
  75.3 0.2 convolution_add_fusion.1
  75.5 2.1 %copy.95 = f32[320,3,64]{0,2,1:T(8,128)} copy(f32[320,3,64]{2,1,0:T(4,128)} %fusion.2) | data formatting | bytes 491520 | tf_op jit(solution)/shard_map/pkgt,pkdt->pkgd/dot_general | solution.py:75
  77.6 1.3 fusion.17
  78.9 0.1 copy.96
  79.0 2.0 %convolution_convert_fusion = bf16[64,1536]{1,0:T(8,128)(2,1)} fusion(bf16[64,192]{0,1:T(8,128)(2,1)S(1)} %bitcast.111, bf16[1,192,1536]{2,1,0:T(8,128)(2,1)} %param.20), kind=kOutput, calls=%fused_computation.13 | convolution fusion | flops 37847040 | bytes 811008 | tf_op jit(solution)/shard_map/dot_general | solution.py:141
  81.0 0.8 copy.97
  82.0 0.2 select_reduce_fusion.4
  82.6 27.9 %reduce-scatter.2.cloned.1.call-done = bf16[8,1536]{1,0:T(8,128)(2,1)} async-done(((bf16[64,1536]{1,0:T(8,128)(2,1)}), bf16[8,1536]{1,0:T(8,128)(2,1)}) %reduce-scatter.2.cloned.1.call-update) | async-done | bytes 24592 | tf_op jit(solution)/shard_map/reduce_scatter | solution.py:140
  110.5 0.9 fusion.41
  111.5 0.9 fusion.59
  112.4 0.6 gather_fusion
  113.2 0.3 convolution_convert_fusion.1
  113.5 0.7 reshape.281
  114.1 6.8 %all-to-all-start = ((bf16[16,2,1,1536]{3,1,2,0:T(2,128)(2,1)}), bf16[16,2,1,1536]{3,1,2,0:T(2,128)(2,1)S(1)}, u32[]{:S(2)}, u32[]{:S(2)}) async-start(bf16[16,2,1,1536]{3,1,2,0:T(2,128)(2,1)} %bitcast.28), calls=%async_computation.1 | async-start | bytes 196608 | tf_op jit(solution)/shard_map/all_to_all | solution.py:176
  120.9 0.1 divide_reduce_fusion
  121.1 7.7 %all-to-all-done = bf16[16,2,1,1536]{3,1,2,0:T(2,128)(2,1)S(1)} async-done(((bf16[16,2,1,1536]{3,1,2,0:T(2,128)(2,1)}), bf16[16,2,1,1536]{3,1,2,0:T(2,128)(2,1)S(1)}, u32[]{:S(2)}, u32[]{:S(2)}) %all-to-all-start) | async-done | bytes 98336 | tf_op jit(solution)/shard_map/all_to_all | solution.py:176
  128.8 4.0 %fusion.8 = f32[1,32,2048]{2,1,0:T(8,128)S(1)} fusion(bf16[32,1536]{1,0:T(8,128)(2,1)S(1)} %reshape.282, bf16[1,1536,2048]{2,1,0:T(8,128)(2,1)} %param.24), kind=kOutput, calls=%fused_computation.14 | convolution fusion | flops 201326592 | bytes 6651904 | tf_op jit(solution)/shard_map/erd,edf->erf/dot_general | solution.py:98
  132.8 0.6 fusion.11
  133.4 0.7 transpose_reshape.3
  134.1 3.5 %all-to-all-start.1 = ((bf16[16,2,1,1536]{3,1,2,0:T(2,128)(2,1)}), bf16[16,2,1,1536]{3,1,2,0:T(2,128)(2,1)S(1)}, u32[]{:S(2)}, u32[]{:S(2)}) async-start(bf16[16,2,1,1536]{3,1,2,0:T(2,128)(2,1)} %bitcast.33), calls=%async_computation.2 | async-start | bytes 196608 | tf_op jit(solution)/shard_map/all_to_all | solution.py:177
  137.7 7.6 %all-to-all-done.1 = bf16[16,2,1,1536]{3,1,2,0:T(2,128)(2,1)S(1)} async-done(((bf16[16,2,1,1536]{3,1,2,0:T(2,128)(2,1)}), bf16[16,2,1,1536]{3,1,2,0:T(2,128)(2,1)S(1)}, u32[]{:S(2)}, u32[]{:S(2)}) %all-to-all-start.1) | async-done | bytes 98336 | tf_op jit(solution)/shard_map/all_to_all | solution.py:177
  145.4 0.2 fusion.16
  145.6 0.6 fusion.44
  (41 shorter events, 1.3 us)
Async XLA Ops:
  6.5 126.2 %copy-start = (bf16[1,1024,1536]{2,1,0:T(8,128)(2,1)S(1)}, bf16[1,1024,1536]{2,1,0:T(8,128)(2,1)}, u32[]{:S(2)}) copy-start(bf16[1,1024,1536]{2,1,0:T(8,128)(2,1)} %param.25) | copy-start | bytes 9437188
  6.5 104.0 %reduce-scatter.2.cloned.1.call-start = ((), (), s32[]{:S(2)}) async-start(), calls=%async_computation.3 | async-start | bytes 221184 | tf_op jit(solution)/shard_map/reduce_scatter | solution.py:140
  57.5 0.9 copy-start.1
  58.4 8.0 %slice-start = ((bf16[64,1,320]{2,0,1:T(8,128)(2,1)}), bf16[64,1,192]{2,0,1:T(8,128)(2,1)S(1)}, s32[]{:S(2)}) async-start(bf16[64,1,320]{2,0,1:T(8,128)(2,1)} %copy-done.1), calls=%async_computation.4 | async-start | bytes 65536 | tf_op jit(solution)/shard_map/slice | solution.py:25
  59.4 7.0 %copy-start.3 = (f32[64,64]{1,0:T(8,128)S(1)}, f32[64,64]{1,0:T(8,128)}, u32[]{:S(2)}) copy-start(f32[64,64]{1,0:T(8,128)} %get-tuple-element.8) | copy-start | bytes 49156
  59.5 6.8 %copy-start.2 = (pred[320,128]{1,0:T(8,128)(4,1)}, pred[320,128]{1,0:T(8,128)(4,1)S(1)}, u32[]{:S(2)}) copy-start(pred[320,128]{1,0:T(8,128)(4,1)S(1)} %add_compare_fusion) | copy-start | bytes 122884
  68.7 42.6 %copy-start.4 = (f32[1536]{0:T(1024)S(1)}, f32[1536]{0:T(1024)}, u32[]{:S(2)}) copy-start(f32[1536]{0:T(1024)} %param.21) | copy-start | bytes 18436
  114.1 14.6 %all-to-all-start = ((bf16[16,2,1,1536]{3,1,2,0:T(2,128)(2,1)}), bf16[16,2,1,1536]{3,1,2,0:T(2,128)(2,1)S(1)}, u32[]{:S(2)}, u32[]{:S(2)}) async-start(bf16[16,2,1,1536]{3,1,2,0:T(2,128)(2,1)} %bitcast.28), calls=%async_computation.1 | async-start | bytes 196608 | tf_op jit(solution)/shard_map/all_to_all | solution.py:176
  134.1 11.3 %all-to-all-start.1 = ((bf16[16,2,1,1536]{3,1,2,0:T(2,128)(2,1)}), bf16[16,2,1,1536]{3,1,2,0:T(2,128)(2,1)S(1)}, u32[]{:S(2)}, u32[]{:S(2)}) async-start(bf16[16,2,1,1536]{3,1,2,0:T(2,128)(2,1)} %bitcast.33), calls=%async_computation.2 | async-start | bytes 196608 | tf_op jit(solution)/shard_map/all_to_all | solution.py:177
Sparse Core Ops, SparseCore 0:
  81.1 29.3 reduce-scatter.1
where the time goes:
time: 154 us; the launch traced here: 153 us
  waiting for transfers between devices  43.2 us (28%)
  blocking collectives  40.8 us (26%)
  matrix products  24.8 us (16%)
  between operations  13.6 us (9%)
  local copies, waits for them, and re-layouts  11.7 us (8%)
  starting transfers between devices  10.3 us (7%)
  other arithmetic  8.5 us (6%)
    reduce_scatter x1, waiting for transfers between devices, shards(): lax.psum_scatter(jnp.dot(head_out, out_flat, preferred_element_type=jnp.f...  27.9 us
    all_gather x1, blocking collectives, shards(): every_row = lax.all_gather(hidden, 'req', axis=0, tiled=True)  26.8 us
    all_gather x1, blocking collectives, shards(): tokens = lax.all_gather(picked_rows, 'kv', axis=1, tiled=True)  14 us
    all_to_all x1, waiting for transfers between devices, shards(): lax.all_to_all(outgoing, 'req', split_axis=0, concat_axis=0, tiled=True)  7.69 us
    all_to_all x1, waiting for transfers between devices, shards(): lax.all_to_all(expert_apply(arrived, gate_up, down), 'req', split_axis=0,...  7.62 us
    all_to_all x1, starting transfers between devices, shards(): lax.all_to_all(outgoing, 'req', split_axis=0, concat_axis=0, tiled=True)  6.8 us
    dot_general x1, matrix products, attend(): jnp.einsum('pkgt,pkdt->pkgd', weights.astype(jnp.bfloat16), kv_cache[:, :...  6.5 us
    dot_general x1, matrix products, attend(): jnp.einsum('pkgd,pkdt->pkgt', page_queries, kv_cache[:, :, :head_dim, :],...  5.63 us
  transfers between devices with their start and end apart: 3, of which 3 were waited for; matrix products, arithmetic and copies ran while one was open for 1% of the time, Pallas kernels for 0%

commit v1 on v0

--- a/solution.py
+++ b/solution.py
@@ -1,11 +1,32 @@
+import functools
 import jax
 import jax.numpy as jnp
 from jax import lax
 from jax.sharding import PartitionSpec as P
+from jax.lax import axis_index, axis_size, ppermute
 
 REQ_DEV = 64
 NEG_FILL = -1e30
 EPS_NORM = 1e-05
+
+
+def fill_the_masks(slab_in, comm_axis, row_dim):
+    p_count = axis_size(comm_axis)
+    windows = []
+    for k in tuple(range(p_count)):
+        windows.append((k, (k + 1) % p_count))
+    small = [None] * p_count
+    small[p_count - 1] = slab_in
+    for p in range(p_count - 2, -1, -1):
+        small[p] = ppermute(small[p + 1], comm_axis, windows)
+    front = jnp.concatenate(small, axis=row_dim)
+    v_now = axis_index(comm_axis)
+    current_block = (v_now + 1) * slab_in.shape[row_dim]
+    odd = jnp.roll(front, current_block, axis=row_dim)
+    return odd
+
+
+_unite_floor = functools.partial(fill_the_masks, comm_axis="kv", row_dim=1)
 
 
 def rms_norm(values, gain_vec):
@@ -131,7 +152,7 @@
     picked_rows = jnp.dot(pick, every_row, preferred_element_type=jnp.float32).astype(
         every_row.dtype
     )
-    tokens = lax.all_gather(picked_rows, "kv", axis=1, tiled=True)
+    tokens = _unite_floor(picked_rows)
     normed = rms_norm(tokens, attn_gain)
     head_out = attend(normed, seq_lens, page_table, kv_cache, qkv_weight)
     sub_rows = routes.shape[0]

time: 154 us -> 179 us (1.16)
  waiting for transfers between devices: 43.2 us -> 65.5 us
  blocking collectives: 40.8 us -> 27 us
  local copies, waits for them, and re-layouts: 11.7 us -> 18.2 us
  other arithmetic: 8.5 us -> 14.8 us
  matrix products: 24.8 us -> 27.6 us
    ppermute x0 -> x7, waiting for transfers between devices: none -> 24.5 us  [fill_the_masks(): small[p] = ppermute(small[p + 1], comm_axis, windows)]
    all_gather x1 -> x0, blocking collectives: 14 us -> none  [shards(): tokens = lax.all_gather(picked_rows, 'kv', axis=1, tiled=True)]
    reduce_scatter x1, waiting for transfers between devices: 27.9 us -> 25.6 us  [shards(): lax.psum_scatter(jnp.dot(head_out, out_flat, preferred_element_type=jnp.f...]
    unnamed x15 -> x40, local copies, waits for them, and re-layouts: 3.09 us -> 5.14 us
  transfers between devices with their start and end apart: 3 -> 10, of which waited for: 3 -> 10; matrix products, arithmetic and copies ran while one was open for 1% -> 5% of each run, Pallas kernels for 0% -> 0%
where the time goes in v1:
time: 179 us; the launch traced here: 177 us
  waiting for transfers between devices  65.5 us (37%)
  matrix products  27.6 us (15%)
  blocking collectives  27 us (15%)
  local copies, waits for them, and re-layouts  18.2 us (10%)
  other arithmetic  14.8 us (8%)
  between operations  13.7 us (8%)
  starting transfers between devices  10.3 us (6%)
    all_gather x1, blocking collectives, shards(): every_row = lax.all_gather(hidden, 'req', axis=0, tiled=True)  27 us
    reduce_scatter x1, waiting for transfers between devices, shards(): lax.psum_scatter(jnp.dot(head_out, out_flat, preferred_element_type=jnp.f...  25.6 us
    ppermute x7, waiting for transfers between devices, fill_the_masks(): small[p] = ppermute(small[p + 1], comm_axis, windows)  24.5 us
    all_to_all x1, waiting for transfers between devices, shards(): lax.all_to_all(outgoing, 'req', split_axis=0, concat_axis=0, tiled=True)  7.69 us
    all_to_all x1, waiting for transfers between devices, shards(): lax.all_to_all(expert_apply(arrived, gate_up, down), 'req', split_axis=0,...  7.62 us
    all_to_all x1, starting transfers between devices, shards(): lax.all_to_all(outgoing, 'req', split_axis=0, concat_axis=0, tiled=True)  6.8 us
    dot_general x1, matrix products, attend(): jnp.einsum('pkgt,pkdt->pkgd', weights.astype(jnp.bfloat16), kv_cache[:, :...  6.57 us
    dot_general x1, matrix products, attend(): jnp.einsum('pkgd,pkdt->pkgt', page_queries, kv_cache[:, :, :head_dim, :],...  5.62 us
  transfers between devices with their start and end apart: 10, of which 10 were waited for; matrix products, arithmetic and copies ran while one was open for 5% of the time, Pallas kernels for 0%

profile of v1, /device:TPU:0, one launch (start us, length us, event | category | flops | bytes accessed | tf_op | source)
XLA Modules:
  0.0 177.2 jit_solution(10668790227598191121)
XLA Ops:
  6.5 27.0 %all_gather.3 = bf16[1024,192]{1,0:T(8,128)(2,1)} all-gather(bf16[64,192]{1,0:T(8,128)(2,1)} %param.13), channel_id=1, replica_groups=mesh['req'=16,'kv'=8] {'req'}, dimensions={0}, use_global_device_ids=true | all-gather | bytes 417792 | tf_op jit(solution)/shard_map/all_gather | solution.py:147
  33.6 0.8 dynamic_slice.10
  34.3 1.3 convolution_convert_fusion.3
  35.7 0.8 copy.84
  37.2 0.8 select_reduce_fusion
  38.1 2.1 %collective-permute-done = bf16[64,192]{1,0:T(8,128)(2,1)S(1)} collective-permute-done((bf16[64,192]{1,0:T(8,128)(2,1)S(1)}, bf16[64,192]{1,0:T(8,128)(2,1)S(1)}, u32[]{:S(2)}, u32[]{:S(2)}) %collective-permute-start) | collective-permute-done | bytes 24608 | tf_op jit(solution)/shard_map/ppermute | solution.py:21
  40.2 0.9 fusion.7
  41.1 3.6 %collective-permute-done.1 = bf16[64,192]{1,0:T(8,128)(2,1)S(1)} collective-permute-done((bf16[64,192]{1,0:T(8,128)(2,1)S(1)}, bf16[64,192]{1,0:T(8,128)(2,1)S(1)}, u32[]{:S(2)}, u32[]{:S(2)}) %collective-permute-start.1) | collective-permute-done | bytes 24608 | tf_op jit(solution)/shard_map/ppermute | solution.py:21
  44.8 0.8 select_reduce_fusion.3
  45.5 3.8 %collective-permute-done.2 = bf16[64,192]{1,0:T(8,128)(2,1)S(1)} collective-permute-done((bf16[64,192]{1,0:T(8,128)(2,1)S(1)}, bf16[64,192]{1,0:T(8,128)(2,1)S(1)}, u32[]{:S(2)}, u32[]{:S(2)}) %collective-permute-start.2) | collective-permute-done | bytes 24608 | tf_op jit(solution)/shard_map/ppermute | solution.py:21
  49.3 0.8 add_compare_fusion
  50.1 0.8 copy.93
  50.9 2.9 %collective-permute-done.3 = bf16[64,192]{1,0:T(8,128)(2,1)S(1)} collective-permute-done((bf16[64,192]{1,0:T(8,128)(2,1)S(1)}, bf16[64,192]{1,0:T(8,128)(2,1)S(1)}, u32[]{:S(2)}, u32[]{:S(2)}) %collective-permute-start.3) | collective-permute-done | bytes 24608 | tf_op jit(solution)/shard_map/ppermute | solution.py:21
  54.0 4.4 %collective-permute-done.4 = bf16[64,192]{1,0:T(8,128)(2,1)S(1)} collective-permute-done((bf16[64,192]{1,0:T(8,128)(2,1)S(1)}, bf16[64,192]{1,0:T(8,128)(2,1)S(1)}, u32[]{:S(2)}, u32[]{:S(2)}) %collective-permute-start.4) | collective-permute-done | bytes 24608 | tf_op jit(solution)/shard_map/ppermute | solution.py:21
  58.7 4.3 %collective-permute-done.5 = bf16[64,192]{1,0:T(8,128)(2,1)S(1)} collective-permute-done((bf16[64,192]{1,0:T(8,128)(2,1)S(1)}, bf16[64,192]{1,0:T(8,128)(2,1)S(1)}, u32[]{:S(2)}, u32[]{:S(2)}) %collective-permute-start.5) | collective-permute-done | bytes 24608 | tf_op jit(solution)/shard_map/ppermute | solution.py:21
  64.3 3.3 %collective-permute-done.6 = bf16[64,192]{1,0:T(8,128)(2,1)} collective-permute-done((bf16[64,192]{1,0:T(8,128)(2,1)S(1)}, bf16[64,192]{1,0:T(8,128)(2,1)}, u32[]{:S(2)}, u32[]{:S(2)}) %collective-permute-start.6) | collective-permute-done | bytes 24608 | tf_op jit(solution)/shard_map/ppermute | solution.py:21
  67.6 1.2 concatenate.6
  69.1 1.7 convolution_bitcast_fusion
  70.8 0.7 fusion.45
  72.1 1.6 convolution_convert_fusion.2
  73.7 1.4 copy.111
  75.1 1.5 copy.110
  76.6 1.8 %copy.86 = bf16[320,3,64]{2,1,0:T(4,128)(2,1)} copy(bf16[320,3,64]{0,2,1:T(8,128)(2,1)} %bitcast.94) | data formatting | bytes 245760 | tf_op jit(solution)/shard_map/reshape.5
  78.5 5.6 %fusion.55 = (f32[320,3]{1,0:T(8,128)}, f32[320,3,128]{2,1,0:T(4,128)}) fusion(bf16[320,3,64]{2,1,0:T(4,128)(2,1)} %copy.86, bf16[320,1,128,128]{3,2,0,1:T(8,128)(2,1)} %bitcast.97, pred[320,128]{1,0:T(8,128)(4,1)} %add_compare_fusion), kind=kOutput, calls=%fused_computation.101 | convolution fusion | flops 16096320 | bytes 6106880 | tf_op jit(solution)/shard_map/pkgd,pkdt->pkgt/dot_general | solution.py:73
  84.1 1.0 copy.87
  85.1 0.9 select_reduce_fusion.2
  86.0 0.8 multiply_reduce_fusion
  87.4 0.8 select_reduce_fusion.1
  88.2 0.8 copy.89
  89.1 2.0 %fusion.21 = f32[320,3]{1,0:T(8,128)S(1)} fusion(f32[320,3,128]{2,1,0:T(4,128)} %get-tuple-element.14, f32[320,3]{1,0:T(8,128)} %copy.89, pred[320,128]{1,0:T(8,128)(4,1)} %add_compare_fusion), kind=kLoop, calls=%fused_computation.33 | loop fusion | flops 367680 | bytes 540160 | tf_op jit(solution)/shard_map/reduce_sum | solution.py:95
  91.0 6.6 %fusion.2 = f32[320,3,64]{2,1,0:T(4,128)} fusion(bf16[320,1,128,128]{3,2,0,1:T(8,128)(2,1)} %bitcast.98, f32[320,3,128]{2,1,0:T(4,128)} %get-tuple-element.14, f32[320,3]{1,0:T(8,128)} %copy.89, pred[320,128]{1,0:T(8,128)(4,1)} %add_compare_fusion), kind=kOutput, calls=%fused_computation.4 | convolution fusion | flops 16097280 | bytes 6348800 | tf_op jit(solution)/shard_map/pkgt,pkdt->pkgd/dot_general | solution.py:96
  97.6 0.9 convolution_add_fusion.1
  98.5 2.0 %copy.91 = f32[320,3,64]{0,2,1:T(8,128)} copy(f32[320,3,64]{2,1,0:T(4,128)} %fusion.2) | data formatting | bytes 491520 | tf_op jit(solution)/shard_map/pkgt,pkdt->pkgd/dot_general | solution.py:96
  100.5 1.9 %fusion.17 = bf16[64,3,64]{2,0,1:T(8,128)(2,1)} fusion(f32[320,3,64]{0,2,1:T(8,128)} %copy.91, pred[64,320]{1,0:T(8,128)(4,1)} %copy-done.1, f32[64,3]{0,1:T(4,128)} %convolution_add_fusion.1, f32[64,64]{1,0:T(8,128)} %get-tuple-element.7, f32[64,3]{0,1:T(4,128)S(1)} %bitcast_convert_fusion), kind=kOutput, calls=%fused_computation.24 | convolution fusion | flops 47235072 | bytes 308736 | tf_op jit(solution)/shard_map/dot_general | solution.py:106
  102.4 1.5 copy.92
  103.9 2.0 %convolution_convert_fusion = bf16[64,1536]{1,0:T(8,128)(2,1)} fusion(bf16[64,192]{0,1:T(8,128)(2,1)} %bitcast.95, bf16[1,192,1536]{2,1,0:T(8,128)(2,1)} %param.20), kind=kOutput, calls=%fused_computation.13 | convolution fusion | flops 37847040 | bytes 811008 | tf_op jit(solution)/shard_map/dot_general | solution.py:162
  106.0 0.7 bitcast_or_fusion
  106.9 0.7 multiply_add_fusion.1
  107.6 25.6 %reduce-scatter.2.cloned.1.call-done = bf16[8,1536]{1,0:T(8,128)(2,1)} async-done(((bf16[64,1536]{1,0:T(8,128)(2,1)}), bf16[8,1536]{1,0:T(8,128)(2,1)}) %reduce-scatter.2.cloned.1.call-update) | async-done | bytes 24592 | tf_op jit(solution)/shard_map/reduce_scatter | solution.py:161
  133.2 0.9 fusion.40
  134.7 0.8 fusion.42
  135.5 0.9 fusion.57
  138.2 6.8 %all-to-all-start = ((bf16[16,2,1,1536]{3,1,2,0:T(2,128)(2,1)}), bf16[16,2,1,1536]{3,1,2,0:T(2,128)(2,1)S(1)}, u32[]{:S(2)}, u32[]{:S(2)}) async-start(bf16[16,2,1,1536]{3,1,2,0:T(2,128)(2,1)} %bitcast.24), calls=%async_computation.1 | async-start | bytes 196608 | tf_op jit(solution)/shard_map/all_to_all | solution.py:197
  145.1 7.7 %all-to-all-done = bf16[16,2,1,1536]{3,1,2,0:T(2,128)(2,1)S(1)} async-done(((bf16[16,2,1,1536]{3,1,2,0:T(2,128)(2,1)}), bf16[16,2,1,1536]{3,1,2,0:T(2,128)(2,1)S(1)}, u32[]{:S(2)}, u32[]{:S(2)}) %all-to-all-start) | async-done | bytes 98336 | tf_op jit(solution)/shard_map/all_to_all | solution.py:197
  152.9 4.0 %fusion.8 = f32[1,32,2048]{2,1,0:T(8,128)S(1)} fusion(bf16[32,1536]{1,0:T(8,128)(2,1)S(1)} %reshape.282, bf16[1,1536,2048]{2,1,0:T(8,128)(2,1)} %param.24), kind=kOutput, calls=%fused_computation.14 | convolution fusion | flops 201326592 | bytes 6651904 | tf_op jit(solution)/shard_map/erd,edf->erf/dot_general | solution.py:119
  157.5 0.7 transpose_reshape.3
  158.1 3.5 %all-to-all-start.1 = ((bf16[16,2,1,1536]{3,1,2,0:T(2,128)(2,1)}), bf16[16,2,1,1536]{3,1,2,0:T(2,128)(2,1)S(1)}, u32[]{:S(2)}, u32[]{:S(2)}) async-start(bf16[16,2,1,1536]{3,1,2,0:T(2,128)(2,1)} %bitcast.29), calls=%async_computation.2 | async-start | bytes 196608 | tf_op jit(solution)/shard_map/all_to_all | solution.py:198
  161.8 7.6 %all-to-all-done.1 = bf16[16,2,1,1536]{3,1,2,0:T(2,128)(2,1)S(1)} async-done(((bf16[16,2,1,1536]{3,1,2,0:T(2,128)(2,1)}), bf16[16,2,1,1536]{3,1,2,0:T(2,128)(2,1)S(1)}, u32[]{:S(2)}, u32[]{:S(2)}) %all-to-all-start.1) | async-done | bytes 98336 | tf_op jit(solution)/shard_map/all_to_all | solution.py:198
  (78 shorter events, 8.4 us)
Async XLA Ops:
  6.5 150.3 %copy-start = (bf16[1,1024,1536]{2,1,0:T(8,128)(2,1)S(1)}, bf16[1,1024,1536]{2,1,0:T(8,128)(2,1)}, u32[]{:S(2)}) copy-start(bf16[1,1024,1536]{2,1,0:T(8,128)(2,1)} %param.25) | copy-start | bytes 9437188
  6.5 126.7 %reduce-scatter.2.cloned.1.call-start = ((), (), s32[]{:S(2)}) async-start(), calls=%async_computation.3 | async-start | bytes 221184 | tf_op jit(solution)/shard_map/reduce_scatter | solution.py:161
  35.6 28.6 %copy-start.3 = (bf16[64,192]{1,0:T(8,128)(2,1)}, bf16[64,192]{1,0:T(8,128)(2,1)S(1)}, u32[]{:S(2)}) copy-start(bf16[64,192]{1,0:T(8,128)(2,1)S(1)} %convolution_convert_fusion.3) | copy-start | bytes 73732
  35.6 4.6 %collective-permute-start = (bf16[64,192]{1,0:T(8,128)(2,1)S(1)}, bf16[64,192]{1,0:T(8,128)(2,1)S(1)}, u32[]{:S(2)}, u32[]{:S(2)}) collective-permute-start(bf16[64,192]{1,0:T(8,128)(2,1)S(1)} %convolution_convert_fusion.3), channel_id=1, source_target_pairs={{0,1},{1,2},{2,3},{3,4},{4,5},{5,6},{6,7},{7,0},{8,9},{9,10},{10,1... | collective-permute-start | bytes 73736 | tf_op jit(solution)/shard_map/ppermute | solution.py:21
  40.2 24.0 %copy-start.6 = (bf16[64,192]{1,0:T(8,128)(2,1)}, bf16[64,192]{1,0:T(8,128)(2,1)S(1)}, u32[]{:S(2)}) copy-start(bf16[64,192]{1,0:T(8,128)(2,1)S(1)} %collective-permute-done) | copy-start | bytes 73732
  40.2 4.6 %collective-permute-start.1 = (bf16[64,192]{1,0:T(8,128)(2,1)S(1)}, bf16[64,192]{1,0:T(8,128)(2,1)S(1)}, u32[]{:S(2)}, u32[]{:S(2)}) collective-permute-start(bf16[64,192]{1,0:T(8,128)(2,1)S(1)} %collective-permute-done), channel_id=1, source_target_pairs={{0,1},{1,2},{2,3},{3,4},{4,5},{5,6},{6,7},{7,0},{8,9},{9,10},{10,1... | collective-permute-start | bytes 73736 | tf_op jit(solution)/shard_map/ppermute | solution.py:21
  41.1 3.6 %copy-start.1 = (pred[64,320]{1,0:T(8,128)(4,1)}, pred[64,320]{1,0:T(8,128)(4,1)S(1)}, u32[]{:S(2)}) copy-start(pred[64,320]{1,0:T(8,128)(4,1)S(1)} %fusion.7) | copy-start | bytes 61444
  44.8 0.8 copy-start.7
  44.8 4.6 %collective-permute-start.2 = (bf16[64,192]{1,0:T(8,128)(2,1)S(1)}, bf16[64,192]{1,0:T(8,128)(2,1)S(1)}, u32[]{:S(2)}, u32[]{:S(2)}) collective-permute-start(bf16[64,192]{1,0:T(8,128)(2,1)S(1)} %collective-permute-done.1), channel_id=1, source_target_pairs={{0,1},{1,2},{2,3},{3,4},{4,5},{5,6},{6,7},{7,0},{8,9},{9,10},{10,1... | collective-permute-start | bytes 73736 | tf_op jit(solution)/shard_map/ppermute | solution.py:21
  49.3 14.9 %copy-start.8 = (bf16[64,192]{1,0:T(8,128)(2,1)}, bf16[64,192]{1,0:T(8,128)(2,1)S(1)}, u32[]{:S(2)}) copy-start(bf16[64,192]{1,0:T(8,128)(2,1)S(1)} %collective-permute-done.2) | copy-start | bytes 73732
  49.3 4.6 %collective-permute-start.3 = (bf16[64,192]{1,0:T(8,128)(2,1)S(1)}, bf16[64,192]{1,0:T(8,128)(2,1)S(1)}, u32[]{:S(2)}, u32[]{:S(2)}) collective-permute-start(bf16[64,192]{1,0:T(8,128)(2,1)S(1)} %collective-permute-done.2), channel_id=1, source_target_pairs={{0,1},{1,2},{2,3},{3,4},{4,5},{5,6},{6,7},{7,0},{8,9},{9,10},{10,1... | collective-permute-start | bytes 73736 | tf_op jit(solution)/shard_map/ppermute | solution.py:21
  50.9 13.3 %copy-start.15 = (s32[16]{0:T(128)}, s32[16]{0:T(128)S(1)}, u32[]{:S(2)}) copy-start(s32[16]{0:T(128)S(1)} %eq.87) | copy-start | bytes 196
  53.9 10.4 %copy-start.9 = (bf16[64,192]{1,0:T(8,128)(2,1)}, bf16[64,192]{1,0:T(8,128)(2,1)S(1)}, u32[]{:S(2)}) copy-start(bf16[64,192]{1,0:T(8,128)(2,1)S(1)} %collective-permute-done.3) | copy-start | bytes 73732
  53.9 4.6 %collective-permute-start.4 = (bf16[64,192]{1,0:T(8,128)(2,1)S(1)}, bf16[64,192]{1,0:T(8,128)(2,1)S(1)}, u32[]{:S(2)}, u32[]{:S(2)}) collective-permute-start(bf16[64,192]{1,0:T(8,128)(2,1)S(1)} %collective-permute-done.3), channel_id=1, source_target_pairs={{0,1},{1,2},{2,3},{3,4},{4,5},{5,6},{6,7},{7,0},{8,9},{9,10},{10,1... | collective-permute-start | bytes 73736 | tf_op jit(solution)/shard_map/ppermute | solution.py:21
  58.4 5.8 %copy-start.10 = (bf16[64,192]{1,0:T(8,128)(2,1)}, bf16[64,192]{1,0:T(8,128)(2,1)S(1)}, u32[]{:S(2)}) copy-start(bf16[64,192]{1,0:T(8,128)(2,1)S(1)} %collective-permute-done.4) | copy-start | bytes 73732
  58.4 4.6 %collective-permute-start.5 = (bf16[64,192]{1,0:T(8,128)(2,1)S(1)}, bf16[64,192]{1,0:T(8,128)(2,1)S(1)}, u32[]{:S(2)}, u32[]{:S(2)}) collective-permute-start(bf16[64,192]{1,0:T(8,128)(2,1)S(1)} %collective-permute-done.4), channel_id=1, source_target_pairs={{0,1},{1,2},{2,3},{3,4},{4,5},{5,6},{6,7},{7,0},{8,9},{9,10},{10,1... | collective-permute-start | bytes 73736 | tf_op jit(solution)/shard_map/ppermute | solution.py:21
  58.6 5.7 %copy-start.17 = (s32[16]{0:T(128)}, s32[16]{0:T(128)S(1)}, u32[]{:S(2)}) copy-start(s32[16]{0:T(128)S(1)} %select_reduce_fusion.4) | copy-start | bytes 196
  63.0 1.3 copy-start.11
  63.0 4.7 %collective-permute-start.6 = (bf16[64,192]{1,0:T(8,128)(2,1)S(1)}, bf16[64,192]{1,0:T(8,128)(2,1)}, u32[]{:S(2)}, u32[]{:S(2)}) collective-permute-start(bf16[64,192]{1,0:T(8,128)(2,1)S(1)} %collective-permute-done.5), channel_id=1, source_target_pairs={{0,1},{1,2},{2,3},{3,4},{4,5},{5,6},{6,7},{7,0},{8,9},{9,10},{10,1... | collective-permute-start | bytes 73736 | tf_op jit(solution)/shard_map/ppermute | solution.py:21
  86.8 0.6 copy-start.12
  89.0 8.6 %copy-start.2 = (pred[64,320]{1,0:T(8,128)(4,1)S(1)}, pred[64,320]{1,0:T(8,128)(4,1)}, u32[]{:S(2)}) copy-start(pred[64,320]{1,0:T(8,128)(4,1)} %copy-done.1) | copy-start | bytes 61444
  89.0 8.6 %copy-start.13 = (f32[64,3]{0,1:T(4,128)S(1)}, f32[64,3]{0,1:T(4,128)}, u32[]{:S(2)}) copy-start(f32[64,3]{0,1:T(4,128)} %copy-done.12) | copy-start | bytes 2308
  89.0 11.4 %copy-start.16 = (bf16[64,1,3]{0,2,1:T(4,128)(2,1)S(1)}, bf16[64,1,3]{0,2,1:T(4,128)(2,1)}, u32[]{:S(2)}) copy-start(bf16[64,1,3]{0,2,1:T(4,128)(2,1)} %get-tuple-element.11) | copy-start | bytes 1156
  89.0 17.8 %copy-start.14 = (s32[8,2]{1,0:T(8,128)S(1)}, s32[8,2]{1,0:T(8,128)}, u32[]{:S(2)}) copy-start(s32[8,2]{1,0:T(8,128)} %get-tuple-element.9) | copy-start | bytes 196
  134.1 0.6 copy-start.4
  138.2 14.6 %all-to-all-start = ((bf16[16,2,1,1536]{3,1,2,0:T(2,128)(2,1)}), bf16[16,2,1,1536]{3,1,2,0:T(2,128)(2,1)S(1)}, u32[]{:S(2)}, u32[]{:S(2)}) async-start(bf16[16,2,1,1536]{3,1,2,0:T(2,128)(2,1)} %bitcast.24), calls=%async_computation.1 | async-start | bytes 196608 | tf_op jit(solution)/shard_map/all_to_all | solution.py:197
  152.9 16.8 %copy-start.5 = (bf16[8,1536]{1,0:T(8,128)(2,1)S(1)}, bf16[8,1536]{1,0:T(8,128)(2,1)}, u32[]{:S(2)}) copy-start(bf16[8,1536]{1,0:T(8,128)(2,1)} %copy-done.4) | copy-start | bytes 73732
  158.1 11.3 %all-to-all-start.1 = ((bf16[16,2,1,1536]{3,1,2,0:T(2,128)(2,1)}), bf16[16,2,1,1536]{3,1,2,0:T(2,128)(2,1)S(1)}, u32[]{:S(2)}, u32[]{:S(2)}) async-start(bf16[16,2,1,1536]{3,1,2,0:T(2,128)(2,1)} %bitcast.29), calls=%async_computation.2 | async-start | bytes 196608 | tf_op jit(solution)/shard_map/all_to_all | solution.py:198
Sparse Core Ops, SparseCore 0:
  106.1 27.0 reduce-scatter.1
